TPU v7x, 128 devices: a whole 4x4x4 slice. The times are simulated.
128 devices in a mesh: req: 8 (over x, core), mlp: 16 (over y, z).
Axes of the slice: x: 4, y: 4, z: 4, core: 2. Of those that a mesh axis runs over, the one named last changes fastest.
Arguments:
- hidden_in: bfloat16 [16384, 2560], P(('req', 'mlp')), may hold values from -6 to 6
- queries: bfloat16 [16384, 2048], P(('req', 'mlp')), may hold values from -120 to 120
- keys_new: bfloat16 [16384, 512], P(('req', 'mlp')), may hold values from -4.4 to 4.4
- values_new: bfloat16 [16384, 512], P(('req', 'mlp')), may hold values from -5 to 5
- keys_cache: bfloat16 [4096, 512], P('req'), may hold values from -4.4 to 4.4
- values_cache: bfloat16 [4096, 512], P('req'), may hold values from -5 to 5
- out_weight: bfloat16 [2048, 2560], replicated, may hold values from -0.375 to 0.375
- norm_gain: float32 [2560], replicated, may hold values from 0.25 to 1.75
- gate_weight: bfloat16 [2560, 9728], P(None, 'mlp'), may hold values from -0.125 to 0.125
- up_weight: bfloat16 [2560, 9728], P(None, 'mlp'), may hold values from -0.125 to 0.125
- down_weight: bfloat16 [9728, 2560], P('mlp'), may hold values from -0.0625 to 0.0625
- lengths: int32 [8, 16], P('req', 'mlp'), may hold values from 1 to 128, 1536 in all within a row
- slot_request: int32 [128], replicated, may hold values from 0 to 127, each once
- cache_group: int32 [8, 4], replicated, may hold values from 0 to 3, each once within a row
Outputs:
- output: bfloat16 [16384, 2560], P(('req', 'mlp'))
Inputs may be any that keep to these rules, and one draw needn't show every extreme that they name: The 16 entries of one row of lengths sum to 1536, and one of them is 128. `slot_request`: each request appears in one slot. `cache_group`: each row names every group once.
All inputs are finite; a program needn't handle non-finite values. No bound on the sum of `lengths` on one device may be relied on, other than what follows from the above.
Results may differ from a plain program's by a relative error of at most 0.014.
Values may be sent and summed in bfloat16 or wider, within the bound.
No kernel may reach another device: no remote copies, remote signals or barrier semaphores. Data moves between devices by JAX's collectives and lax.ppermute only.
A program may use at most 128 MiB of HBM per device.

v0:
```python
import jax
import jax.numpy as jnp
from jax import lax
from jax.sharding import PartitionSpec as P

HEADS = 16
KVH = 4
HD = 128
GROUPS = 4
NEGATIVE = -1e30
EPSILON = 1e-06


def partial_attention(query_block, key_rows, value_rows, allowed):
    row_count = query_block.shape[0]
    key_count = key_rows.shape[0]
    per_group = HEADS // KVH
    query_heads = query_block.reshape(row_count, KVH, per_group, HD)
    key_heads = key_rows.reshape(key_count, KVH, HD)
    value_heads = value_rows.reshape(key_count, KVH, HD)
    scores = jnp.einsum(
        "tkgd,skd->kgts", query_heads, key_heads, preferred_element_type=jnp.float32
    ) * HD ** (-0.5)
    if allowed is not None:
        scores = jnp.where(allowed, scores, NEGATIVE)
    maxima = jnp.max(scores, axis=3)
    weights = jnp.exp(scores - maxima[..., None])
    totals = jnp.sum(weights, axis=3)
    context = jnp.einsum(
        "kgts,skd->tkgd",
        weights.astype(jnp.bfloat16),
        value_heads,
        preferred_element_type=jnp.float32,
    )
    context = context.reshape(row_count, HEADS * HD)
    maxima = jnp.transpose(maxima, (2, 0, 1)).reshape(row_count, HEADS)
    totals = jnp.transpose(totals, (2, 0, 1)).reshape(row_count, HEADS)
    return (context, maxima, totals)


def merge_pair(earlier, latest):
    context_early, maxima_early, totals_early = earlier
    context_late, maxima_late, totals_late = latest
    row_count = context_early.shape[0]
    highest = jnp.maximum(maxima_early, maxima_late)
    factor_early = jnp.exp(maxima_early - highest)
    factor_late = jnp.exp(maxima_late - highest)
    context = (
        context_early.reshape(row_count, HEADS, HD) * factor_early[..., None]
        + context_late.reshape(row_count, HEADS, HD) * factor_late[..., None]
    )
    return (
        context.reshape(row_count, HEADS * HD),
        highest,
        totals_early * factor_early + totals_late * factor_late,
    )


def shards(
    hidden_in,
    queries,
    keys_new,
    values_new,
    keys_cache,
    values_cache,
    out_weight,
    norm_gain,
    gate_weight,
    up_weight,
    down_weight,
    lengths,
    slot_request,
    cache_group,
):
    owners = lax.axis_size("req")
    columns = lax.axis_size("mlp")
    owner_index = lax.axis_index("req")
    column_index = lax.axis_index("mlp")
    tokens = queries.shape[0]
    width_kv = keys_cache.shape[1]
    piece_rows = keys_cache.shape[0] // GROUPS
    slot_group = slot_request // (slot_request.shape[0] // GROUPS)
    own_row = cache_group[owner_index]
    wanted = lax.dynamic_slice_in_dim(slot_group.reshape(owners, columns), column_index, 1, 1)[:, 0]
    group_ids = jnp.arange(GROUPS, dtype=jnp.int32)
    sub_block = jnp.sum(
        jnp.where(own_row[None, :] == wanted[:, None], group_ids[None, :], 0), axis=1
    )
    slab_keys = keys_cache.reshape(GROUPS, piece_rows, width_kv)
    slab_values = values_cache.reshape(GROUPS, piece_rows, width_kv)
    positions = jnp.arange(tokens, dtype=jnp.int32)
    causal = positions[:, None] >= positions[None, :]
    local_part = partial_attention(queries, keys_new, values_new, causal)
    send_keys = jnp.take(slab_keys, sub_block, axis=0)
    send_values = jnp.take(slab_values, sub_block, axis=0)
    got_keys, got_values = (
        lax.all_to_all(send_keys, "req", split_axis=0, concat_axis=0, tiled=True),
        lax.all_to_all(send_values, "req", split_axis=0, concat_axis=0, tiled=True),
    )
    prefix_part = partial_attention(
        queries,
        got_keys.reshape(owners * piece_rows, width_kv),
        got_values.reshape(owners * piece_rows, width_kv),
        None,
    )
    context, highest, totals = merge_pair(local_part, prefix_part)
    context = context.reshape(tokens, HEADS, HD)
    context = (context / totals[..., None]).reshape(tokens, HEADS * HD).astype(jnp.bfloat16)
    attended = jnp.dot(context, out_weight, preferred_element_type=jnp.float32)
    residual = (hidden_in.astype(jnp.float32) + attended).astype(jnp.bfloat16)
    widened = residual.astype(jnp.float32)
    normed = (
        widened
        * lax.rsqrt(jnp.mean(widened * widened, axis=1, keepdims=True) + EPSILON)
        * norm_gain[None, :]
    ).astype(jnp.bfloat16)
    shard_rows = lax.all_gather(normed, "mlp", axis=0, tiled=True)
    gate_values = jnp.dot(shard_rows, gate_weight, preferred_element_type=jnp.float32)
    upward = jnp.dot(shard_rows, up_weight, preferred_element_type=jnp.float32)
    hidden = (jax.nn.silu(gate_values) * upward).astype(jnp.bfloat16)
    partial_terms = jnp.dot(hidden, down_weight, preferred_element_type=jnp.float32)
    mixed = lax.psum_scatter(
        partial_terms.astype(jnp.bfloat16), "mlp", scatter_dimension=0, tiled=True
    ).astype(jnp.float32)
    result = residual.astype(jnp.float32) + mixed
    live_slot = positions[:, None] < lengths[0, 0]
    return jnp.where(live_slot, result, 0.0).astype(jnp.bfloat16)


def solution(mesh):
    return jax.shard_map(
        shards,
        mesh=mesh,
        in_specs=(
            P(("req", "mlp"), None),
            P(("req", "mlp"), None),
            P(("req", "mlp"), None),
            P(("req", "mlp"), None),
            P("req", None),
            P("req", None),
            P(),
            P(),
            P(None, "mlp"),
            P(None, "mlp"),
            P("mlp", None),
            P("req", "mlp"),
            P(),
            P(),
        ),
        out_specs=P(("req", "mlp"), None),
        check_vma=False,
    )
```

profile of v0, /device:TPU:0, one launch (start us, length us, event | category | flops | bytes accessed | tf_op | source)
XLA Modules:
  0.0 287.3 jit_solution(5620928909980571331)
XLA Ops:
  6.5 0.0 copy-start
  6.5 0.8 and_select_fusion
  7.4 0.1 reshape.109
  7.4 0.2 dynamic-slice_reduce_fusion
  7.6 0.9 dynamic-slice_reduce_fusion.1
  8.5 0.1 select_reduce_fusion
  8.6 2.6 gather_fusion
  11.2 0.0 copy-start.6
  11.2 0.0 copy-start.7
  11.2 2.7 gather_fusion.1
  13.9 3.1 %broadcast_select_fusion = (bf16[8,128,512]{2,1,0:T(8,128)(2,1)}, bf16[8,128,512]{2,1,0:T(8,128)(2,1)}) fusion(bf16[8,128,512]{2,1,0:T(8,128)(2,1)} %gather_fusion.1, pred[8]{0:T(512)(128)(4,1)S(1)} %compare_and_fusion, bf16[8,128,512]{2,1,0:T(8,128)(2,1)} %gather_fusion), kind=kLoop, calls=%fused_computation.31 | loop fusion | flops 1048576 | bytes 4194312 | tf_op jit(solution)/shard_map/jit(_take)/select_n | solution.py:95
  17.0 4.4 %all-to-all-start = ((bf16[8,128,512]{2,1,0:T(8,128)(2,1)}), bf16[8,128,512]{2,1,0:T(8,128)(2,1)}, u32[]{:S(2)}, u32[]{:S(2)}) async-start(bf16[8,128,512]{2,1,0:T(8,128)(2,1)} %get-tuple-element.10), calls=%async_computation | async-start | bytes 2097152 | tf_op jit(solution)/shard_map/all_to_all | solution.py:97
  21.4 2.2 reshape.105
  23.6 0.0 copy-done.6
  23.7 0.0 copy-done.7
  23.7 0.1 copy.55
  23.8 1.4 fusion.32
  25.2 0.2 fusion.18
  25.4 1.4 fusion.20
  26.8 10.7 %all-to-all-done = bf16[8,128,512]{2,1,0:T(8,128)(2,1)} async-done(((bf16[8,128,512]{2,1,0:T(8,128)(2,1)}), bf16[8,128,512]{2,1,0:T(8,128)(2,1)}, u32[]{:S(2)}, u32[]{:S(2)}) %all-to-all-start) | async-done | bytes 1048608 | tf_op jit(solution)/shard_map/all_to_all | solution.py:97
  37.5 4.2 %all-to-all-start.1 = ((bf16[8,128,512]{2,1,0:T(8,128)(2,1)}), bf16[8,128,512]{2,1,0:T(8,128)(2,1)}, u32[]{:S(2)}, u32[]{:S(2)}) async-start(bf16[8,128,512]{2,1,0:T(8,128)(2,1)} %get-tuple-element.9), calls=%async_computation.1 | async-start | bytes 2097152 | tf_op jit(solution)/shard_map/all_to_all | solution.py:98
  41.7 0.0 all-gather.2.cloned.1.call-start
  41.8 2.2 reshape.140
  44.0 2.6 bitcast_reduce_fusion
  46.6 0.0 copy-start.2
  46.6 3.2 %copy-done.2 = f32[4,1024,128,4]{2,1,3,0:T(8,128)} copy-done((f32[4,1024,128,4]{2,1,3,0:T(8,128)}, f32[4,1024,128,4]{2,1,3,0:T(8,128)S(1)}, u32[]{:S(2)}) %copy-start.2) | copy-done | bytes 8388632
  49.8 1.4 fusion.1
  51.3 6.4 %all-to-all-done.1 = bf16[8,128,512]{2,1,0:T(8,128)(2,1)} async-done(((bf16[8,128,512]{2,1,0:T(8,128)(2,1)}), bf16[8,128,512]{2,1,0:T(8,128)(2,1)}, u32[]{:S(2)}, u32[]{:S(2)}) %all-to-all-start.1) | async-done | bytes 1048608 | tf_op jit(solution)/shard_map/all_to_all | solution.py:98
  57.7 2.1 reshape.141
  59.8 5.4 %fusion.3 = f32[4,128,4,128]{3,1,2,0:T(8,128)S(1)} fusion(f32[4,1024,128,4]{2,1,3,0:T(8,128)} %copy-done.2, f32[4,4,128]{2,1,0:T(4,128)S(1)} %get-tuple-element.11, bf16[1024,4,128,1]{2,1,0,3:T(4,128)(2,1)} %bitcast.68), kind=kOutput, calls=%fused_computation.9 | convolution fusion | flops 543162368 | bytes 10493952 | tf_op jit(solution)/shard_map/kgts,skd->tkgd/dot_general | solution.py:29
  65.2 0.0 copy-done.4
  65.2 0.2 fusion.14
  65.4 0.0 copy-done.5
  65.4 0.0 copy-start.8
  65.5 5.6 %multiply_reduce_fusion = (f32[128]{0:T(128)S(1)}, f32[128,2560]{1,0:T(8,128)S(1)}) fusion(bf16[128,2048]{0,1:T(8,128)(2,1)S(1)} %fusion.14, bf16[2048,2560]{1,0:T(8,128)(2,1)} %param.22, bf16[128,2560]{1,0:T(8,128)(2,1)S(1)} %copy-done.5), kind=kOutput, calls=%fused_computation.21 | convolution fusion | flops 1344143232 | bytes 12976640 | tf_op jit(solution)/shard_map/dot_general | solution.py:109
  71.1 1.1 copy-done.3
  72.2 0.0 copy-done.8
  72.2 1.0 multiply_convert_fusion.1
  73.2 0.0 all-gather.2.cloned.1.call-update
  73.2 0.2 reduce-scatter.2.cloned.1.call-start
  73.4 80.9 %all-gather.2.cloned.1.call-done = bf16[2048,2560]{1,0:T(8,128)(2,1)} async-done(((bf16[128,2560]{1,0:T(8,128)(2,1)}), bf16[2048,2560]{1,0:T(8,128)(2,1)}) %all-gather.2.cloned.1.call-update) | async-done | bytes 10485776 | tf_op jit(solution)/shard_map/all_gather | solution.py:117
  154.3 11.7 %fusion.33 = f32[2048,608]{0,1:T(8,128)} fusion(bf16[2048,2560]{1,0:T(8,128)(2,1)} %all-gather.2.cloned.1.call-done, bf16[2560,608]{0,1:T(8,128)(2,1)} %param.24), kind=kOutput, calls=%fused_computation.61 | convolution fusion | flops 6375342080 | bytes 18579456 | tf_op jit(solution)/shard_map/dot_general | solution.py:118
  166.1 0.0 copy-done
  166.1 21.7 %convolution_convert_fusion = bf16[2048,2560]{1,0:T(8,128)(2,1)} fusion(bf16[608,2560]{1,0:T(8,128)(2,1)S(1)} %copy-done, f32[2048,608]{0,1:T(8,128)} %fusion.33, bf16[2048,2560]{1,0:T(8,128)(2,1)} %all-gather.2.cloned.1.call-done, bf16[2560,608]{0,1:T(8,128)(2,1)} %param.25), kind=kOutput, calls=%fused_computation.2 | convolution fusion | flops 12763398144 | bytes 32178176 | tf_op jit(solution)/shard_map/dot_general | solution.py:121
  187.8 0.0 reduce-scatter.2.cloned.1.call-update
  188.6 89.3 %reduce-scatter.2.cloned.1.call-done = bf16[128,2560]{1,0:T(8,128)(2,1)} async-done(((bf16[2048,2560]{1,0:T(8,128)(2,1)}), bf16[128,2560]{1,0:T(8,128)(2,1)}) %reduce-scatter.2.cloned.1.call-update) | async-done | bytes 655376 | tf_op jit(solution)/shard_map/reduce_scatter | solution.py:122
  278.0 2.5 select_convert_fusion
  280.5 0.0 copy-done.1
  (12 shorter events, 0.1 us)
Async XLA Ops:
  6.5 159.5 %copy-start = (bf16[608,2560]{1,0:T(8,128)(2,1)S(1)}, bf16[608,2560]{1,0:T(8,128)(2,1)}, u32[]{:S(2)}) copy-start(bf16[608,2560]{1,0:T(8,128)(2,1)} %param.26) | copy-start | bytes 9338884
  11.2 12.4 %copy-start.6 = (bf16[128,512]{1,0:T(8,128)(2,1)S(1)}, bf16[128,512]{1,0:T(8,128)(2,1)}, u32[]{:S(2)}) copy-start(bf16[128,512]{1,0:T(8,128)(2,1)} %param.18) | copy-start | bytes 393220
  11.2 12.4 %copy-start.7 = (bf16[128,512]{1,0:T(8,128)(2,1)S(1)}, bf16[128,512]{1,0:T(8,128)(2,1)}, u32[]{:S(2)}) copy-start(bf16[128,512]{1,0:T(8,128)(2,1)} %param.19) | copy-start | bytes 393220
  17.0 20.5 %all-to-all-start = ((bf16[8,128,512]{2,1,0:T(8,128)(2,1)}), bf16[8,128,512]{2,1,0:T(8,128)(2,1)}, u32[]{:S(2)}, u32[]{:S(2)}) async-start(bf16[8,128,512]{2,1,0:T(8,128)(2,1)} %get-tuple-element.10), calls=%async_computation | async-start | bytes 2097152 | tf_op jit(solution)/shard_map/all_to_all | solution.py:97
  37.5 20.2 %all-to-all-start.1 = ((bf16[8,128,512]{2,1,0:T(8,128)(2,1)}), bf16[8,128,512]{2,1,0:T(8,128)(2,1)}, u32[]{:S(2)}, u32[]{:S(2)}) async-start(bf16[8,128,512]{2,1,0:T(8,128)(2,1)} %get-tuple-element.9), calls=%async_computation.1 | async-start | bytes 2097152 | tf_op jit(solution)/shard_map/all_to_all | solution.py:98
  41.7 112.6 %all-gather.2.cloned.1.call-start = ((), (), s32[]{:S(2)}) async-start(), calls=%async_computation.3 | async-start | bytes 11141120 | tf_op jit(solution)/shard_map/all_gather | solution.py:117
  46.6 3.2 %copy-start.2 = (f32[4,1024,128,4]{2,1,3,0:T(8,128)}, f32[4,1024,128,4]{2,1,3,0:T(8,128)S(1)}, u32[]{:S(2)}) copy-start(f32[4,1024,128,4]{2,1,3,0:T(8,128)S(1)} %get-tuple-element.12) | copy-start | bytes 25165828
  59.8 5.4 %copy-start.4 = (f32[4,4,128,128]{2,3,1,0:T(8,128)S(1)}, f32[4,4,128,128]{2,3,1,0:T(8,128)}, u32[]{:S(2)}) copy-start(f32[4,4,128,128]{2,3,1,0:T(8,128)} %fusion.20) | copy-start | bytes 3145732
  59.8 5.6 %copy-start.5 = (bf16[128,2560]{1,0:T(8,128)(2,1)S(1)}, bf16[128,2560]{1,0:T(8,128)(2,1)}, u32[]{:S(2)}) copy-start(bf16[128,2560]{1,0:T(8,128)(2,1)} %param.16) | copy-start | bytes 1966084
  65.4 6.7 %copy-start.8 = (f32[2560]{0:T(1024)S(1)}, f32[2560]{0:T(1024)}, u32[]{:S(2)}) copy-start(f32[2560]{0:T(1024)} %param.23) | copy-start | bytes 30724
  71.1 1.1 copy-start.3
  73.2 204.7 %reduce-scatter.2.cloned.1.call-start = ((), (), s32[]{:S(2)}) async-start(), calls=%async_computation.4 | async-start | bytes 11141120 | tf_op jit(solution)/shard_map/reduce_scatter | solution.py:122
  187.8 92.7 %copy-start.1 = (bf16[608,2560]{1,0:T(8,128)(2,1)S(1)}, bf16[608,2560]{1,0:T(8,128)(2,1)}, u32[]{:S(2)}) copy-start(bf16[608,2560]{1,0:T(8,128)(2,1)} %param.26) | copy-start | bytes 9338884
Sparse Core Ops, SparseCore 0:
  73.3 80.9 all-gather.1
  187.9 89.9 reduce-scatter.1
where the time goes:
time: 288 us; the launch traced here: 287 us
  waiting for transfers between devices  187 us (65%)
  matrix products  49.9 us (17%)
  local copies, waits for them, and re-layouts  17.4 us (6%)
  between operations  14.3 us (5%)
  other arithmetic  9.37 us (3%)
  starting transfers between devices  8.92 us (3%)
    reduce_scatter x1, waiting for transfers between devices, shards(): lax.psum_scatter(partial_terms.astype(jnp.bfloat16), 'mlp', scatter_dimen...  89.3 us
    all_gather x1, waiting for transfers between devices, shards(): shard_rows = lax.all_gather(normed, 'mlp', axis=0, tiled=True)  80.9 us
    dot_general x1, matrix products, shards(): jnp.dot(hidden, down_weight, preferred_element_type=jnp.float32)  21.7 us
    dot_general x1, matrix products, shards(): jnp.dot(shard_rows, gate_weight, preferred_element_type=jnp.float32)  11.7 us
    all_to_all x1, waiting for transfers between devices, shards(): lax.all_to_all(send_keys, 'req', split_axis=0, concat_axis=0, tiled=True)  10.7 us
    dot_general x2, matrix products, partial_attention(): jnp.einsum('kgts,skd->tkgd', weights.astype(jnp.bfloat16), value_heads, p...  6.77 us
    all_to_all x1, waiting for transfers between devices, shards(): lax.all_to_all(send_values, 'req', split_axis=0, concat_axis=0, tiled=True)  6.41 us
  transfers between devices with their start and end apart: 4, of which 4 were waited for; matrix products, arithmetic and copies ran while one was open for 4% of the time, Pallas kernels for 0%

commit v1 on v0

--- a/solution.py
+++ b/solution.py
@@ -9,6 +9,22 @@
 GROUPS = 4
 NEGATIVE = -1e30
 EPSILON = 1e-06
+
+
+def ring_gather(x, axis, dim):
+    ways, here, step = (lax.axis_size(axis), lax.axis_index(axis), x.shape[dim])
+    lengths = [n * ways if d == dim else n for d, n in enumerate(x.shape)]
+    full = lax.dynamic_update_slice_in_dim(jnp.zeros(lengths, x.dtype), x, here * step, axis=dim)
+    going_up = going_down = x
+    for far in range(1, ways // 2 + 1):
+        going_up = lax.ppermute(going_up, axis, [(d, (d + 1) % ways) for d in range(ways)])
+        full = lax.dynamic_update_slice_in_dim(full, going_up, (here - far) % ways * step, axis=dim)
+        if 2 * far < ways:
+            going_down = lax.ppermute(going_down, axis, [(d, (d - 1) % ways) for d in range(ways)])
+            full = lax.dynamic_update_slice_in_dim(
+                full, going_down, (here + far) % ways * step, axis=dim
+            )
+    return full
 
 
 def partial_attention(query_block, key_rows, value_rows, allowed):
@@ -114,7 +130,7 @@
         * lax.rsqrt(jnp.mean(widened * widened, axis=1, keepdims=True) + EPSILON)
         * norm_gain[None, :]
     ).astype(jnp.bfloat16)
-    shard_rows = lax.all_gather(normed, "mlp", axis=0, tiled=True)
+    shard_rows = ring_gather(normed, "mlp", 0)
     gate_values = jnp.dot(shard_rows, gate_weight, preferred_element_type=jnp.float32)
     upward = jnp.dot(shard_rows, up_weight, preferred_element_type=jnp.float32)
     hidden = (jax.nn.silu(gate_values) * upward).astype(jnp.bfloat16)

time: 288 us -> 343 us (1.19)
  starting transfers between devices: 8.92 us -> 47.2 us
  local copies, waits for them, and re-layouts: 17.4 us -> 36.4 us
    ppermute x0 -> x15, waiting for transfers between devices: none -> 83.1 us  [the longest x8 83.1 us: ring_gather(): lax.ppermute(going_up, axis, [(d, (d + 1) % ways) for d in range(ways)])]
    all_gather x1 -> x0, waiting for transfers between devices: 80.9 us -> none  [shards(): shard_rows = lax.all_gather(normed, 'mlp', axis=0, tiled=True)]
    ppermute x0 -> x15, starting transfers between devices: none -> 38.6 us  [the longest x7 36.6 us: ring_gather(): lax.ppermute(going_down, axis, [(d, (d - 1) % ways) for d in range(ways)])]
    dynamic_update_slice x0 -> x15, local copies, waits for them, and re-layouts: none -> 15.5 us  [the longest x8 8.22 us: ring_gather(): lax.dynamic_update_slice_in_dim(full, going_up, (here - far) % ways * ste...]
    broadcast_in_dim x0 -> x1, local copies, waits for them, and re-layouts: none -> 4.5 us  [ring_gather(): jnp.zeros(lengths, x.dtype)]
    reduce_scatter x1, waiting for transfers between devices: 89.3 us -> 85.5 us  [shards(): lax.psum_scatter(partial_terms.astype(jnp.bfloat16), 'mlp', scatter_dimen...]
  transfers between devices with their start and end apart: 4 -> 18, of which waited for: 4 -> 11; matrix products, arithmetic and copies ran while one was open for 4% -> 8% of each run, Pallas kernels for 0% -> 0%
where the time goes in v1:
time: 343 us; the launch traced here: 342 us
  waiting for transfers between devices  186 us (54%)
  matrix products  49 us (14%)
  starting transfers between devices  47.2 us (14%)
  local copies, waits for them, and re-layouts  36.4 us (11%)
  between operations  14.2 us (4%)
  other arithmetic  9.61 us (3%)
    reduce_scatter x1, waiting for transfers between devices, shards(): lax.psum_scatter(partial_terms.astype(jnp.bfloat16), 'mlp', scatter_dimen...  85.5 us
    ppermute x8, waiting for transfers between devices, ring_gather(): lax.ppermute(going_up, axis, [(d, (d + 1) % ways) for d in range(ways)])  83.1 us
    ppermute x7, starting transfers between devices, ring_gather(): lax.ppermute(going_down, axis, [(d, (d - 1) % ways) for d in range(ways)])  36.6 us
    dot_general x1, matrix products, shards(): jnp.dot(hidden, down_weight, preferred_element_type=jnp.float32)  21.7 us
    dot_general x1, matrix products, shards(): jnp.dot(shard_rows, gate_weight, preferred_element_type=jnp.float32)  10.9 us
    all_to_all x1, waiting for transfers between devices, shards(): lax.all_to_all(send_keys, 'req', split_axis=0, concat_axis=0, tiled=True)  10.7 us
    dynamic_update_slice x8, local copies, waits for them, and re-layouts, ring_gather(): lax.dynamic_update_slice_in_dim(full, going_up, (here - far) % ways * ste...  8.22 us
    dynamic_update_slice x7, local copies, waits for them, and re-layouts, ring_gather(): lax.dynamic_update_slice_in_dim(full, going_down, (here + far) % ways * s...  7.31 us
  transfers between devices with their start and end apart: 18, of which 11 were waited for; matrix products, arithmetic and copies ran while one was open for 8% of the time, Pallas kernels for 0%

profile of v1, /device:TPU:0, one launch (start us, length us, event | category | flops | bytes accessed | tf_op | source)
XLA Modules:
  0.0 342.2 jit_solution(5613128402806919337)
XLA Ops:
  8.6 2.6 gather_fusion
  11.3 2.6 gather_fusion.1
  13.9 3.1 broadcast_select_fusion
  17.0 4.4 %all-to-all-start = ((bf16[8,128,512]{2,1,0:T(8,128)(2,1)}), bf16[8,128,512]{2,1,0:T(8,128)(2,1)}, u32[]{:S(2)}, u32[]{:S(2)}) async-start(bf16[8,128,512]{2,1,0:T(8,128)(2,1)} %get-tuple-element.12), calls=%async_computation | async-start | bytes 2097152 | tf_op jit(solution)/shard_map/all_to_all | solution.py:113
  21.4 2.2 reshape.105
  23.8 1.4 fusion.34
  25.3 1.4 fusion.20
  26.7 10.7 %all-to-all-done = bf16[8,128,512]{2,1,0:T(8,128)(2,1)} async-done(((bf16[8,128,512]{2,1,0:T(8,128)(2,1)}), bf16[8,128,512]{2,1,0:T(8,128)(2,1)}, u32[]{:S(2)}, u32[]{:S(2)}) %all-to-all-start) | async-done | bytes 1048608 | tf_op jit(solution)/shard_map/all_to_all | solution.py:113
  37.4 4.2 %all-to-all-start.1 = ((bf16[8,128,512]{2,1,0:T(8,128)(2,1)}), bf16[8,128,512]{2,1,0:T(8,128)(2,1)}, u32[]{:S(2)}, u32[]{:S(2)}) async-start(bf16[8,128,512]{2,1,0:T(8,128)(2,1)} %get-tuple-element.11), calls=%async_computation.1 | async-start | bytes 2097152 | tf_op jit(solution)/shard_map/all_to_all | solution.py:114
  41.7 2.2 reshape.140
  43.9 2.6 bitcast_reduce_fusion
  46.6 3.2 copy-done.1
  49.8 1.4 fusion.1
  51.2 6.4 %all-to-all-done.1 = bf16[8,128,512]{2,1,0:T(8,128)(2,1)} async-done(((bf16[8,128,512]{2,1,0:T(8,128)(2,1)}), bf16[8,128,512]{2,1,0:T(8,128)(2,1)}, u32[]{:S(2)}, u32[]{:S(2)}) %all-to-all-start.1) | async-done | bytes 1048608 | tf_op jit(solution)/shard_map/all_to_all | solution.py:114
  57.6 2.2 reshape.141
  59.8 5.4 %fusion.3 = f32[4,128,4,128]{3,1,2,0:T(8,128)S(1)} fusion(f32[4,1024,128,4]{2,1,3,0:T(8,128)} %copy-done.1, f32[4,4,128]{2,1,0:T(4,128)S(1)} %get-tuple-element.13, bf16[1024,4,128,1]{2,1,0,3:T(4,128)(2,1)} %bitcast.68), kind=kOutput, calls=%fused_computation.9 | convolution fusion | flops 543162368 | bytes 10493952 | tf_op jit(solution)/shard_map/kgts,skd->tkgd/dot_general | solution.py:45
  65.4 5.6 %multiply_reduce_fusion = (f32[128]{0:T(128)S(1)}, f32[128,2560]{1,0:T(8,128)S(1)}) fusion(bf16[128,2048]{0,1:T(8,128)(2,1)S(1)} %fusion.14, bf16[2048,2560]{1,0:T(8,128)(2,1)} %param.22, bf16[128,2560]{1,0:T(8,128)(2,1)S(1)} %copy-done.4), kind=kOutput, calls=%fused_computation.21 | convolution fusion | flops 1344143232 | bytes 12976640 | tf_op jit(solution)/shard_map/dot_general | solution.py:125
  71.1 4.5 %broadcast_in_dim.60 = bf16[2048,2560]{1,0:T(8,128)(2,1)} broadcast(bf16[]{:T(256)} %constant.137.clone.1), dimensions={} | broadcast | bytes 10485762 | tf_op jit(solution)/shard_map/broadcast_in_dim | solution.py:17
  75.6 1.3 constant_dynamic-update-slice_fusion.15
  76.8 1.9 collective-permute-start
  78.7 4.6 %collective-permute-start.1 = (bf16[128,2560]{1,0:T(8,128)(2,1)}, bf16[128,2560]{1,0:T(8,128)(2,1)}, u32[]{:S(2)}, u32[]{:S(2)}) collective-permute-start(bf16[128,2560]{1,0:T(8,128)(2,1)} %get-tuple-element.7), channel_id=1, source_target_pairs={{0,15},{1,0},{2,1},{3,2},{4,3},{5,4},{6,5},{7,6},{8,7},{9,8},{10,9... | collective-permute-start | bytes 1966088 | tf_op jit(solution)/shard_map/ppermute | solution.py:23
  83.3 14.7 %collective-permute-done = bf16[128,2560]{1,0:T(8,128)(2,1)} collective-permute-done((bf16[128,2560]{1,0:T(8,128)(2,1)}, bf16[128,2560]{1,0:T(8,128)(2,1)}, u32[]{:S(2)}, u32[]{:S(2)}) %collective-permute-start) | collective-permute-done | bytes 655392 | tf_op jit(solution)/shard_map/ppermute | solution.py:20
  98.1 5.3 %collective-permute-start.3 = (bf16[128,2560]{1,0:T(8,128)(2,1)}, bf16[128,2560]{1,0:T(8,128)(2,1)S(1)}, u32[]{:S(2)}, u32[]{:S(2)}) collective-permute-start(bf16[128,2560]{1,0:T(8,128)(2,1)} %collective-permute-done.1), channel_id=1, source_target_pairs={{0,15},{1,0},{2,1},{3,2},{4,3},{5,4},{6,5},{7,6},{8,7},{9,8},{10,9... | collective-permute-start | bytes 1966088 | tf_op jit(solution)/shard_map/ppermute | solution.py:23
  103.4 2.0 constant_dynamic-update-slice_fusion.14
  105.4 2.0 constant_dynamic-update-slice_fusion.13
  107.3 9.9 %collective-permute-done.2 = bf16[128,2560]{1,0:T(8,128)(2,1)S(1)} collective-permute-done((bf16[128,2560]{1,0:T(8,128)(2,1)}, bf16[128,2560]{1,0:T(8,128)(2,1)S(1)}, u32[]{:S(2)}, u32[]{:S(2)}) %collective-permute-start.2) | collective-permute-done | bytes 655392 | tf_op jit(solution)/shard_map/ppermute | solution.py:20
  117.2 5.3 %collective-permute-start.5 = (bf16[128,2560]{1,0:T(8,128)(2,1)S(1)}, bf16[128,2560]{1,0:T(8,128)(2,1)S(1)}, u32[]{:S(2)}, u32[]{:S(2)}) collective-permute-start(bf16[128,2560]{1,0:T(8,128)(2,1)S(1)} %collective-permute-done.3), channel_id=1, source_target_pairs={{0,15},{1,0},{2,1},{3,2},{4,3},{5,4},{6,5},{7,6},{8,7},{9,8},{10,9... | collective-permute-start | bytes 1966088 | tf_op jit(solution)/shard_map/ppermute | solution.py:23
  124.3 11.0 %collective-permute-done.4 = bf16[128,2560]{1,0:T(8,128)(2,1)S(1)} collective-permute-done((bf16[128,2560]{1,0:T(8,128)(2,1)S(1)}, bf16[128,2560]{1,0:T(8,128)(2,1)S(1)}, u32[]{:S(2)}, u32[]{:S(2)}) %collective-permute-start.4) | collective-permute-done | bytes 655392 | tf_op jit(solution)/shard_map/ppermute | solution.py:20
  135.3 5.3 %collective-permute-start.7 = (bf16[128,2560]{1,0:T(8,128)(2,1)S(1)}, bf16[128,2560]{1,0:T(8,128)(2,1)S(1)}, u32[]{:S(2)}, u32[]{:S(2)}) collective-permute-start(bf16[128,2560]{1,0:T(8,128)(2,1)S(1)} %collective-permute-done.5), channel_id=1, source_target_pairs={{0,15},{1,0},{2,1},{3,2},{4,3},{5,4},{6,5},{7,6},{8,7},{9,8},{10,9... | collective-permute-start | bytes 1966088 | tf_op jit(solution)/shard_map/ppermute | solution.py:23
  141.5 0.9 constant_dynamic-update-slice_fusion.9
  142.4 10.1 %collective-permute-done.6 = bf16[128,2560]{1,0:T(8,128)(2,1)S(1)} collective-permute-done((bf16[128,2560]{1,0:T(8,128)(2,1)S(1)}, bf16[128,2560]{1,0:T(8,128)(2,1)S(1)}, u32[]{:S(2)}, u32[]{:S(2)}) %collective-permute-start.6) | collective-permute-done | bytes 655392 | tf_op jit(solution)/shard_map/ppermute | solution.py:20
  152.5 5.3 %collective-permute-start.9 = (bf16[128,2560]{1,0:T(8,128)(2,1)S(1)}, bf16[128,2560]{1,0:T(8,128)(2,1)S(1)}, u32[]{:S(2)}, u32[]{:S(2)}) collective-permute-start(bf16[128,2560]{1,0:T(8,128)(2,1)S(1)} %collective-permute-done.7), channel_id=1, source_target_pairs={{0,15},{1,0},{2,1},{3,2},{4,3},{5,4},{6,5},{7,6},{8,7},{9,8},{10,9... | collective-permute-start | bytes 1966088 | tf_op jit(solution)/shard_map/ppermute | solution.py:23
  158.7 0.9 constant_dynamic-update-slice_fusion.7
  159.6 9.2 %collective-permute-done.8 = bf16[128,2560]{1,0:T(8,128)(2,1)S(1)} collective-permute-done((bf16[128,2560]{1,0:T(8,128)(2,1)S(1)}, bf16[128,2560]{1,0:T(8,128)(2,1)S(1)}, u32[]{:S(2)}, u32[]{:S(2)}) %collective-permute-start.8) | collective-permute-done | bytes 655392 | tf_op jit(solution)/shard_map/ppermute | solution.py:20
  168.9 5.3 %collective-permute-start.11 = (bf16[128,2560]{1,0:T(8,128)(2,1)S(1)}, bf16[128,2560]{1,0:T(8,128)(2,1)S(1)}, u32[]{:S(2)}, u32[]{:S(2)}) collective-permute-start(bf16[128,2560]{1,0:T(8,128)(2,1)S(1)} %collective-permute-done.9), channel_id=1, source_target_pairs={{0,15},{1,0},{2,1},{3,2},{4,3},{5,4},{6,5},{7,6},{8,7},{9,8},{10,9... | collective-permute-start | bytes 1966088 | tf_op jit(solution)/shard_map/ppermute | solution.py:23
  174.2 0.9 constant_dynamic-update-slice_fusion.6
  176.0 8.4 %collective-permute-done.10 = bf16[128,2560]{1,0:T(8,128)(2,1)S(1)} collective-permute-done((bf16[128,2560]{1,0:T(8,128)(2,1)S(1)}, bf16[128,2560]{1,0:T(8,128)(2,1)S(1)}, u32[]{:S(2)}, u32[]{:S(2)}) %collective-permute-start.10) | collective-permute-done | bytes 655392 | tf_op jit(solution)/shard_map/ppermute | solution.py:20
  184.4 5.3 %collective-permute-start.13 = (bf16[128,2560]{1,0:T(8,128)(2,1)S(1)}, bf16[128,2560]{1,0:T(8,128)(2,1)S(1)}, u32[]{:S(2)}, u32[]{:S(2)}) collective-permute-start(bf16[128,2560]{1,0:T(8,128)(2,1)S(1)} %collective-permute-done.11), channel_id=1, source_target_pairs={{0,15},{1,0},{2,1},{3,2},{4,3},{5,4},{6,5},{7,6},{8,7},{9,8},{10,9... | collective-permute-start | bytes 1966088 | tf_op jit(solution)/shard_map/ppermute | solution.py:23
  189.7 0.9 constant_dynamic-update-slice_fusion.4
  190.6 0.9 constant_dynamic-update-slice_fusion.3
  191.5 7.7 %collective-permute-done.12 = bf16[128,2560]{1,0:T(8,128)(2,1)S(1)} collective-permute-done((bf16[128,2560]{1,0:T(8,128)(2,1)S(1)}, bf16[128,2560]{1,0:T(8,128)(2,1)S(1)}, u32[]{:S(2)}, u32[]{:S(2)}) %collective-permute-start.12) | collective-permute-done | bytes 655392 | tf_op jit(solution)/shard_map/ppermute | solution.py:20
  199.2 0.9 constant_dynamic-update-slice_fusion.2
  201.0 12.1 %collective-permute-done.14 = bf16[128,2560]{1,0:T(8,128)(2,1)S(1)} collective-permute-done((bf16[128,2560]{1,0:T(8,128)(2,1)S(1)}, bf16[128,2560]{1,0:T(8,128)(2,1)S(1)}, u32[]{:S(2)}, u32[]{:S(2)}) %collective-permute-start.14) | collective-permute-done | bytes 655392 | tf_op jit(solution)/shard_map/ppermute | solution.py:20
  213.2 0.9 constant_dynamic-update-slice_fusion
  214.1 10.9 %fusion.37 = f32[2048,608]{0,1:T(8,128)} fusion(bf16[2048,2560]{1,0:T(8,128)(2,1)} %constant_dynamic-update-slice_fusion, bf16[2560,608]{0,1:T(8,128)(2,1)S(1)} %copy-done.8), kind=kOutput, calls=%fused_computation.80 | convolution fusion | flops 6375342080 | bytes 18579456 | tf_op jit(solution)/shard_map/dot_general | solution.py:134
  225.0 21.7 %convolution_convert_fusion = bf16[2048,2560]{1,0:T(8,128)(2,1)} fusion(bf16[608,2560]{1,0:T(8,128)(2,1)S(1)} %copy-done, f32[2048,608]{0,1:T(8,128)} %fusion.37, bf16[2048,2560]{1,0:T(8,128)(2,1)} %constant_dynamic-update-slice_fusion, bf16[2560,608]{0,1:T(8,128)(2,1)} %param.25), kind=kOutput, calls=%fused_computation.2 | convolution fusion | flops 12763398144 | bytes 32178176 | tf_op jit(solution)/shard_map/dot_general | solution.py:137
  247.3 85.5 %reduce-scatter.2.cloned.1.call-done = bf16[128,2560]{1,0:T(8,128)(2,1)} async-done(((bf16[2048,2560]{1,0:T(8,128)(2,1)}), bf16[128,2560]{1,0:T(8,128)(2,1)}) %reduce-scatter.2.cloned.1.call-update) | async-done | bytes 655376 | tf_op jit(solution)/shard_map/reduce_scatter | solution.py:138
  332.8 2.5 select_convert_fusion
  (55 shorter events, 8.0 us)
Async XLA Ops:
  6.5 218.4 %copy-start = (bf16[608,2560]{1,0:T(8,128)(2,1)S(1)}, bf16[608,2560]{1,0:T(8,128)(2,1)}, u32[]{:S(2)}) copy-start(bf16[608,2560]{1,0:T(8,128)(2,1)} %param.26) | copy-start | bytes 9338884
  6.5 17.0 %copy-start.5 = (bf16[128,512]{1,0:T(8,128)(2,1)S(1)}, bf16[128,512]{1,0:T(8,128)(2,1)}, u32[]{:S(2)}) copy-start(bf16[128,512]{1,0:T(8,128)(2,1)} %param.18) | copy-start | bytes 393220
  6.5 17.1 %copy-start.6 = (bf16[128,512]{1,0:T(8,128)(2,1)S(1)}, bf16[128,512]{1,0:T(8,128)(2,1)}, u32[]{:S(2)}) copy-start(bf16[128,512]{1,0:T(8,128)(2,1)} %param.19) | copy-start | bytes 393220
  17.0 20.5 %all-to-all-start = ((bf16[8,128,512]{2,1,0:T(8,128)(2,1)}), bf16[8,128,512]{2,1,0:T(8,128)(2,1)}, u32[]{:S(2)}, u32[]{:S(2)}) async-start(bf16[8,128,512]{2,1,0:T(8,128)(2,1)} %get-tuple-element.12), calls=%async_computation | async-start | bytes 2097152 | tf_op jit(solution)/shard_map/all_to_all | solution.py:113
  37.4 20.2 %all-to-all-start.1 = ((bf16[8,128,512]{2,1,0:T(8,128)(2,1)}), bf16[8,128,512]{2,1,0:T(8,128)(2,1)}, u32[]{:S(2)}, u32[]{:S(2)}) async-start(bf16[8,128,512]{2,1,0:T(8,128)(2,1)} %get-tuple-element.11), calls=%async_computation.1 | async-start | bytes 2097152 | tf_op jit(solution)/shard_map/all_to_all | solution.py:114
  41.7 291.2 %reduce-scatter.2.cloned.1.call-start = ((), (), s32[]{:S(2)}) async-start(), calls=%async_computation.3 | async-start | bytes 11141120 | tf_op jit(solution)/shard_map/reduce_scatter | solution.py:138
  46.5 3.2 copy-start.1
  59.8 5.4 %copy-start.3 = (f32[4,4,128,128]{2,3,1,0:T(8,128)S(1)}, f32[4,4,128,128]{2,3,1,0:T(8,128)}, u32[]{:S(2)}) copy-start(f32[4,4,128,128]{2,3,1,0:T(8,128)} %fusion.20) | copy-start | bytes 3145732
  59.8 5.6 %copy-start.4 = (bf16[128,2560]{1,0:T(8,128)(2,1)S(1)}, bf16[128,2560]{1,0:T(8,128)(2,1)}, u32[]{:S(2)}) copy-start(bf16[128,2560]{1,0:T(8,128)(2,1)} %param.16) | copy-start | bytes 1966084
  65.4 10.2 %copy-start.7 = (f32[2560]{0:T(1024)S(1)}, f32[2560]{0:T(1024)}, u32[]{:S(2)}) copy-start(f32[2560]{0:T(1024)} %param.23) | copy-start | bytes 30724
  71.0 4.5 %copy-start.2 = (f32[128,2560]{1,0:T(8,128)}, f32[128,2560]{1,0:T(8,128)S(1)}, u32[]{:S(2)}) copy-start(f32[128,2560]{1,0:T(8,128)S(1)} %get-tuple-element.18) | copy-start | bytes 3932164
  76.8 21.2 %collective-permute-start = (bf16[128,2560]{1,0:T(8,128)(2,1)}, bf16[128,2560]{1,0:T(8,128)(2,1)}, u32[]{:S(2)}, u32[]{:S(2)}) collective-permute-start(bf16[128,2560]{1,0:T(8,128)(2,1)} %get-tuple-element.7), channel_id=1, source_target_pairs={{0,1},{1,2},{2,3},{3,4},{4,5},{5,6},{6,7},{7,8},{8,9},{9,10},{10,1... | collective-permute-start | bytes 1966088 | tf_op jit(solution)/shard_map/ppermute | solution.py:20
  78.7 19.3 %collective-permute-start.1 = (bf16[128,2560]{1,0:T(8,128)(2,1)}, bf16[128,2560]{1,0:T(8,128)(2,1)}, u32[]{:S(2)}, u32[]{:S(2)}) collective-permute-start(bf16[128,2560]{1,0:T(8,128)(2,1)} %get-tuple-element.7), channel_id=1, source_target_pairs={{0,15},{1,0},{2,1},{3,2},{4,3},{5,4},{6,5},{7,6},{8,7},{9,8},{10,9... | collective-permute-start | bytes 1966088 | tf_op jit(solution)/shard_map/ppermute | solution.py:23
  83.3 130.8 %copy-start.8 = (bf16[2560,608]{0,1:T(8,128)(2,1)S(1)}, bf16[2560,608]{0,1:T(8,128)(2,1)}, u32[]{:S(2)}) copy-start(bf16[2560,608]{0,1:T(8,128)(2,1)} %param.24) | copy-start | bytes 9338884
  98.1 19.1 %collective-permute-start.2 = (bf16[128,2560]{1,0:T(8,128)(2,1)}, bf16[128,2560]{1,0:T(8,128)(2,1)S(1)}, u32[]{:S(2)}, u32[]{:S(2)}) collective-permute-start(bf16[128,2560]{1,0:T(8,128)(2,1)} %collective-permute-done), channel_id=1, source_target_pairs={{0,1},{1,2},{2,3},{3,4},{4,5},{5,6},{6,7},{7,8},{8,9},{9,10},{10,1... | collective-permute-start | bytes 1966088 | tf_op jit(solution)/shard_map/ppermute | solution.py:20
  98.1 19.1 %collective-permute-start.3 = (bf16[128,2560]{1,0:T(8,128)(2,1)}, bf16[128,2560]{1,0:T(8,128)(2,1)S(1)}, u32[]{:S(2)}, u32[]{:S(2)}) collective-permute-start(bf16[128,2560]{1,0:T(8,128)(2,1)} %collective-permute-done.1), channel_id=1, source_target_pairs={{0,15},{1,0},{2,1},{3,2},{4,3},{5,4},{6,5},{7,6},{8,7},{9,8},{10,9... | collective-permute-start | bytes 1966088 | tf_op jit(solution)/shard_map/ppermute | solution.py:23
  117.2 18.1 %collective-permute-start.4 = (bf16[128,2560]{1,0:T(8,128)(2,1)S(1)}, bf16[128,2560]{1,0:T(8,128)(2,1)S(1)}, u32[]{:S(2)}, u32[]{:S(2)}) collective-permute-start(bf16[128,2560]{1,0:T(8,128)(2,1)S(1)} %collective-permute-done.2), channel_id=1, source_target_pairs={{0,1},{1,2},{2,3},{3,4},{4,5},{5,6},{6,7},{7,8},{8,9},{9,10},{10,1... | collective-permute-start | bytes 1966088 | tf_op jit(solution)/shard_map/ppermute | solution.py:20
  117.2 18.1 %collective-permute-start.5 = (bf16[128,2560]{1,0:T(8,128)(2,1)S(1)}, bf16[128,2560]{1,0:T(8,128)(2,1)S(1)}, u32[]{:S(2)}, u32[]{:S(2)}) collective-permute-start(bf16[128,2560]{1,0:T(8,128)(2,1)S(1)} %collective-permute-done.3), channel_id=1, source_target_pairs={{0,15},{1,0},{2,1},{3,2},{4,3},{5,4},{6,5},{7,6},{8,7},{9,8},{10,9... | collective-permute-start | bytes 1966088 | tf_op jit(solution)/shard_map/ppermute | solution.py:23
  135.3 17.2 %collective-permute-start.6 = (bf16[128,2560]{1,0:T(8,128)(2,1)S(1)}, bf16[128,2560]{1,0:T(8,128)(2,1)S(1)}, u32[]{:S(2)}, u32[]{:S(2)}) collective-permute-start(bf16[128,2560]{1,0:T(8,128)(2,1)S(1)} %collective-permute-done.4), channel_id=1, source_target_pairs={{0,1},{1,2},{2,3},{3,4},{4,5},{5,6},{6,7},{7,8},{8,9},{9,10},{10,1... | collective-permute-start | bytes 1966088 | tf_op jit(solution)/shard_map/ppermute | solution.py:20
  135.3 17.2 %collective-permute-start.7 = (bf16[128,2560]{1,0:T(8,128)(2,1)S(1)}, bf16[128,2560]{1,0:T(8,128)(2,1)S(1)}, u32[]{:S(2)}, u32[]{:S(2)}) collective-permute-start(bf16[128,2560]{1,0:T(8,128)(2,1)S(1)} %collective-permute-done.5), channel_id=1, source_target_pairs={{0,15},{1,0},{2,1},{3,2},{4,3},{5,4},{6,5},{7,6},{8,7},{9,8},{10,9... | collective-permute-start | bytes 1966088 | tf_op jit(solution)/shard_map/ppermute | solution.py:23
  152.5 16.4 %collective-permute-start.8 = (bf16[128,2560]{1,0:T(8,128)(2,1)S(1)}, bf16[128,2560]{1,0:T(8,128)(2,1)S(1)}, u32[]{:S(2)}, u32[]{:S(2)}) collective-permute-start(bf16[128,2560]{1,0:T(8,128)(2,1)S(1)} %collective-permute-done.6), channel_id=1, source_target_pairs={{0,1},{1,2},{2,3},{3,4},{4,5},{5,6},{6,7},{7,8},{8,9},{9,10},{10,1... | collective-permute-start | bytes 1966088 | tf_op jit(solution)/shard_map/ppermute | solution.py:20
  152.5 16.4 %collective-permute-start.9 = (bf16[128,2560]{1,0:T(8,128)(2,1)S(1)}, bf16[128,2560]{1,0:T(8,128)(2,1)S(1)}, u32[]{:S(2)}, u32[]{:S(2)}) collective-permute-start(bf16[128,2560]{1,0:T(8,128)(2,1)S(1)} %collective-permute-done.7), channel_id=1, source_target_pairs={{0,15},{1,0},{2,1},{3,2},{4,3},{5,4},{6,5},{7,6},{8,7},{9,8},{10,9... | collective-permute-start | bytes 1966088 | tf_op jit(solution)/shard_map/ppermute | solution.py:23
  168.8 15.5 %collective-permute-start.10 = (bf16[128,2560]{1,0:T(8,128)(2,1)S(1)}, bf16[128,2560]{1,0:T(8,128)(2,1)S(1)}, u32[]{:S(2)}, u32[]{:S(2)}) collective-permute-start(bf16[128,2560]{1,0:T(8,128)(2,1)S(1)} %collective-permute-done.8), channel_id=1, source_target_pairs={{0,1},{1,2},{2,3},{3,4},{4,5},{5,6},{6,7},{7,8},{8,9},{9,10},{10,1... | collective-permute-start | bytes 1966088 | tf_op jit(solution)/shard_map/ppermute | solution.py:20
  168.9 15.5 %collective-permute-start.11 = (bf16[128,2560]{1,0:T(8,128)(2,1)S(1)}, bf16[128,2560]{1,0:T(8,128)(2,1)S(1)}, u32[]{:S(2)}, u32[]{:S(2)}) collective-permute-start(bf16[128,2560]{1,0:T(8,128)(2,1)S(1)} %collective-permute-done.9), channel_id=1, source_target_pairs={{0,15},{1,0},{2,1},{3,2},{4,3},{5,4},{6,5},{7,6},{8,7},{9,8},{10,9... | collective-permute-start | bytes 1966088 | tf_op jit(solution)/shard_map/ppermute | solution.py:23
  184.4 14.9 %collective-permute-start.12 = (bf16[128,2560]{1,0:T(8,128)(2,1)S(1)}, bf16[128,2560]{1,0:T(8,128)(2,1)S(1)}, u32[]{:S(2)}, u32[]{:S(2)}) collective-permute-start(bf16[128,2560]{1,0:T(8,128)(2,1)S(1)} %collective-permute-done.10), channel_id=1, source_target_pairs={{0,1},{1,2},{2,3},{3,4},{4,5},{5,6},{6,7},{7,8},{8,9},{9,10},{10,1... | collective-permute-start | bytes 1966088 | tf_op jit(solution)/shard_map/ppermute | solution.py:20
  184.4 15.8 %collective-permute-start.13 = (bf16[128,2560]{1,0:T(8,128)(2,1)S(1)}, bf16[128,2560]{1,0:T(8,128)(2,1)S(1)}, u32[]{:S(2)}, u32[]{:S(2)}) collective-permute-start(bf16[128,2560]{1,0:T(8,128)(2,1)S(1)} %collective-permute-done.11), channel_id=1, source_target_pairs={{0,15},{1,0},{2,1},{3,2},{4,3},{5,4},{6,5},{7,6},{8,7},{9,8},{10,9... | collective-permute-start | bytes 1966088 | tf_op jit(solution)/shard_map/ppermute | solution.py:23
  199.2 13.9 %collective-permute-start.14 = (bf16[128,2560]{1,0:T(8,128)(2,1)S(1)}, bf16[128,2560]{1,0:T(8,128)(2,1)S(1)}, u32[]{:S(2)}, u32[]{:S(2)}) collective-permute-start(bf16[128,2560]{1,0:T(8,128)(2,1)S(1)} %collective-permute-done.12), channel_id=1, source_target_pairs={{0,1},{1,2},{2,3},{3,4},{4,5},{5,6},{6,7},{7,8},{8,9},{9,10},{10,1... | collective-permute-start | bytes 1966088 | tf_op jit(solution)/shard_map/ppermute | solution.py:20
Sparse Core Ops, SparseCore 0:
  246.8 85.9 reduce-scatter.1
